TPU v7x, 32 devices: a whole 2x2x4 slice. The times are simulated.
32 devices in a mesh: shots: 4 (over x, core), depth: 8 (over z, y).
Axes of the slice: x: 2, y: 2, z: 4, core: 2. Of those that a mesh axis runs over, the one named last changes fastest.
Arguments:
- forward_prev: float32 [4, 64, 128, 256], P('shots', 'depth'), may hold values from -3 to 3
- forward_now: float32 [4, 64, 128, 256], P('shots', 'depth'), may hold values from -3 to 3
- adjoint_prev: float32 [4, 64, 128, 256], P('shots', 'depth'), may hold values from -3 to 3
- adjoint_now: float32 [4, 64, 128, 256], P('shots', 'depth'), may hold values from -3 to 3
- courant: float32 [64, 128, 256], P('depth'), may hold values from 0.05 to 0.18
- wavelet: float32 [2, 512], replicated, may hold values from -5 to 5
- sign_bits: int32 [4, 512], P('shots'), may hold values from 0 to 1
- source_depth: int32 [512], replicated, may hold values from 0 to 63
- source_cell: int32 [512], replicated, may hold values from 0 to 32767
- receiver_depth: int32 [4096], replicated, may hold values from 0 to 63
- receiver_cell: int32 [4096], replicated, may hold values from 0 to 32767
- residual_traces: float32 [4, 2, 4096], P('shots'), may hold values from -5 to 5
Outputs:
- forward_older: float32 [4, 64, 128, 256], P('shots', 'depth')
- forward_newer: float32 [4, 64, 128, 256], P('shots', 'depth')
- adjoint_older: float32 [4, 64, 128, 256], P('shots', 'depth')
- adjoint_newer: float32 [4, 64, 128, 256], P('shots', 'depth')
- gradient: float32 [64, 128, 256], P(None, ('shots', 'depth'))
All inputs are finite; a program needn't handle non-finite values.
Results may differ from a plain program's by a relative error of at most 0.00002.
Values sent between devices are 32-bit elements; how exact they have to be, the bound alone decides.
No kernel may reach another device: no remote copies, remote signals or barrier semaphores. Data moves between devices by JAX's collectives and lax.ppermute only.
A program may use at most 128 MiB of HBM per device.

v0:
```python
import jax
import jax.numpy as jnp
from jax import lax
from jax.sharding import PartitionSpec as P

STEPS = 2
COEFFS = (-205.0 / 72.0, 8.0 / 5.0, -1.0 / 5.0, 8.0 / 315.0, -1.0 / 560.0)
KERNEL = (1.0 / 16.0, 4.0 / 16.0, 6.0 / 16.0, 4.0 / 16.0, 1.0 / 16.0)


def extended_2(shard, sides, width):
    for axis, dim in sides:
        devices, length = (lax.axis_size(axis), shard.shape[dim])
        up = [(i, (i + 1) % devices) for i in range(devices - 1)]
        down = [(j, i) for i, j in up]
        last = lax.slice_in_dim(shard, length - width, length, axis=dim)
        leading = lax.slice_in_dim(shard, 0, width, axis=dim)
        before = lax.ppermute(last, axis, up)
        after = lax.ppermute(leading, axis, down)
        shard = jnp.concatenate([before, shard, after], axis=dim)
    return shard


def shifted(values, axis, offset):
    size = values.shape[axis]
    width = abs(offset)
    filler = jnp.zeros_like(lax.slice_in_dim(values, 0, width, axis=axis))
    if offset > 0:
        kept = lax.slice_in_dim(values, offset, size, axis=axis)
        return jnp.concatenate([kept, filler], axis=axis)
    kept = lax.slice_in_dim(values, 0, size - width, axis=axis)
    return jnp.concatenate([filler, kept], axis=axis)


def laplace(extended):
    zaxis = extended.ndim - 3
    planes = extended.shape[zaxis] - 8
    core = lax.slice_in_dim(extended, 4, 4 + planes, axis=zaxis)
    total = 3.0 * COEFFS[0] * core
    for k in range(1, 5):
        near = lax.slice_in_dim(extended, 4 + k, 4 + k + planes, axis=zaxis) + lax.slice_in_dim(
            extended, 4 - k, 4 - k + planes, axis=zaxis
        )
        near = near + shifted(core, zaxis + 1, k) + shifted(core, zaxis + 1, -k)
        near = near + shifted(core, zaxis + 2, k) + shifted(core, zaxis + 2, -k)
        total = total + COEFFS[k] * near
    return total


def smooth(values, axis):
    total = KERNEL[2] * values
    for k in (1, 2):
        total = total + KERNEL[2 + k] * (shifted(values, axis, k) + shifted(values, axis, -k))
    return total


def spread(flat, values, first_plane, planes, rows, cols):
    lateral = rows * cols
    limit = planes * lateral
    local = flat - first_plane * lateral
    local = jnp.where((local >= 0) & (local < limit), local, limit)
    grid = jnp.zeros((values.shape[0], limit), jnp.float32).at[:, local].add(values, mode="drop")
    return grid.reshape(values.shape[0], planes, rows, cols)


def on_device(
    forward_prev,
    forward_now,
    adjoint_prev,
    adjoint_now,
    courant,
    wavelet,
    sign_bits,
    source_depth,
    source_cell,
    receiver_depth,
    receiver_cell,
    residual_traces,
):
    planes, rows, cols = courant.shape
    lateral = rows * cols
    source_flat = source_depth * lateral + source_cell
    receiver_flat = receiver_depth * lateral + receiver_cell
    signs = (2 * sign_bits - 1).astype(jnp.float32)
    position = lax.axis_index("depth")
    earlier = jnp.stack([forward_prev, adjoint_prev])
    current = jnp.stack([forward_now, adjoint_now])
    correlation = jnp.zeros((planes, rows, cols), jnp.float32)
    for step in range(STEPS):
        extended = extended_2(current, (("depth", 2),), 4)
        first_plane = position * planes
        forward_part = spread(
            source_flat, signs * wavelet[step][None, :], first_plane, planes, rows, cols
        )
        adjoint_part = spread(
            receiver_flat, residual_traces[:, step, :], first_plane, planes, rows, cols
        )
        fresh = (
            2.0 * current
            - earlier
            + courant * laplace(extended)
            + jnp.stack([forward_part, adjoint_part])
        )
        correlation = correlation + jnp.sum(fresh[0] * fresh[1], axis=0)
        earlier, current = (current, fresh)
    lateral_smooth = smooth(smooth(correlation, 1), 2)
    summed = lax.psum_scatter(lateral_smooth, "shots", scatter_dimension=1, tiled=True)
    columns = lax.all_to_all(summed, "depth", split_axis=1, concat_axis=0, tiled=True)
    gradient = smooth(columns, 0)
    return (earlier[0], current[0], earlier[1], current[1], gradient)


def solution(mesh):
    in_specs = (
        P("shots", "depth", None, None),
        P("shots", "depth", None, None),
        P("shots", "depth", None, None),
        P("shots", "depth", None, None),
        P("depth", None, None),
        P(),
        P("shots", None),
        P(),
        P(),
        P(),
        P(),
        P("shots", None, None),
    )
    out_specs = (
        P("shots", "depth", None, None),
        P("shots", "depth", None, None),
        P("shots", "depth", None, None),
        P("shots", "depth", None, None),
        P(None, ("shots", "depth"), None),
    )
    return jax.shard_map(
        on_device, mesh=mesh, in_specs=in_specs, out_specs=out_specs, check_vma=False
    )
```

profile of v0, /device:TPU:0, one launch (start us, length us, event | category | flops | bytes accessed | tf_op | source)
XLA Modules:
  0.0 237.2 jit_solution(1340536631924805276)
XLA Ops:
  7.2 3.2 %fusion.80 = (f32[2,1,4,128,256]{4,3,2,1,0:T(8,128)}, f32[2,1,4,128,256]{4,3,2,1,0:T(8,128)}) fusion(f32[1,1,8,128,256]{4,3,2,1,0:T(8,128)} %bitcast.23, f32[1,1,8,128,256]{4,3,2,1,0:T(8,128)} %bitcast.35), kind=kLoop, calls=%fused_computation.142 | loop fusion | flops 524288 | bytes 4194304 | tf_op jit(solution)/shard_map/stack | solution.py:87
  11.7 6.5 %collective-permute-start.1 = (f32[2,1,4,128,256]{4,3,2,1,0:T(8,128)}, f32[2,1,4,128,256]{4,3,2,1,0:T(8,128)}, u32[]{:S(2)}, u32[]{:S(2)}) collective-permute-start(f32[2,1,4,128,256]{4,3,2,1,0:T(8,128)} %get-tuple-element.52), channel_id=1, source_target_pairs={{0,1},{1,2},{2,3},{3,4},{4,5},{5,6},{6,7},{8,9},{9,10},{10,11},{11... | collective-permute-start | bytes 3145736 | tf_op jit(solution)/shard_map/ppermute | solution.py:18
  18.2 2.4 %fusion.31 = (f32[2,1,8,127,256]{4,3,2,1,0:T(8,128)}, f32[2,1,8,127,256]{4,3,2,1,0:T(8,128)}) fusion(f32[1,1,8,128,256]{4,3,2,1,0:T(8,128)S(1)} %bitcast.24, f32[1,1,8,128,256]{4,3,2,1,0:T(8,128)S(1)} %bitcast.36), kind=kLoop, calls=%fused_computation.86 | loop fusion | flops 1040384 | bytes 6258688 | tf_op jit(solution)/shard_map/stack | solution.py:87
  20.6 2.7 %fusion.33 = (f32[2,1,8,128,255]{4,3,2,1,0:T(8,128)}, f32[2,1,8,128,255]{4,3,2,1,0:T(8,128)}) fusion(f32[1,1,8,128,256]{4,3,2,1,0:T(8,128)S(1)} %bitcast.25, f32[1,1,8,128,256]{4,3,2,1,0:T(8,128)S(1)} %bitcast.37), kind=kLoop, calls=%fused_computation.88 | loop fusion | flops 1044480 | bytes 6275072 | tf_op jit(solution)/shard_map/stack | solution.py:87
  25.9 22.2 %scatter_custom_fusion.1 = f32[262144]{0:T(1024)S(1)} fusion(s32[4096]{0:T(1024)S(1)} %compare_select_fusion, f32[4096]{0:T(1024)S(1)} %bitcast.53, f32[]{:T(128)} %constant.18.clone.1), kind=kCustom, calls=%fused_computation.155 | custom fusion | flops 4096 | bytes 1048580 | tf_op jit(solution)/shard_map/scatter-add | solution.py:62
  49.4 3.5 %scatter_custom_fusion = f32[262144]{0:T(1024)S(1)} fusion(s32[512]{0:T(512)S(1)} %compare_select_fusion.1, f32[512]{0:T(512)S(1)} %bitcast.55, f32[]{:T(128)} %constant.18.clone.1), kind=kCustom, calls=%fused_computation.157 | custom fusion | flops 512 | bytes 1048580 | tf_op jit(solution)/shard_map/scatter-add | solution.py:62
  54.2 22.2 %scatter_custom_fusion.3 = f32[262144]{0:T(1024)S(1)} fusion(s32[4096]{0:T(1024)S(1)} %compare_select_fusion, f32[4096]{0:T(1024)S(1)} %bitcast.52, f32[]{:T(128)} %constant.18.clone.1), kind=kCustom, calls=%fused_computation.151 | custom fusion | flops 4096 | bytes 1048580 | tf_op jit(solution)/shard_map/scatter-add | solution.py:62
  77.6 3.7 %scatter_custom_fusion.2 = f32[262144]{0:T(1024)S(1)} fusion(s32[512]{0:T(512)S(1)} %compare_select_fusion.1, f32[512]{0:T(512)S(1)} %bitcast.54, f32[]{:T(128)} %constant.18.clone.1), kind=kCustom, calls=%fused_computation.153 | custom fusion | flops 512 | bytes 1048580 | tf_op jit(solution)/shard_map/scatter-add | solution.py:62
  82.6 2.7 %fusion.37 = (f32[2,1,8,128,254]{4,3,2,1,0:T(8,128)}, f32[2,1,8,128,254]{4,3,2,1,0:T(8,128)}) fusion(f32[1,1,8,128,256]{4,3,2,1,0:T(8,128)S(1)} %bitcast.27, f32[1,1,8,128,256]{4,3,2,1,0:T(8,128)S(1)} %bitcast.39), kind=kLoop, calls=%fused_computation.92 | loop fusion | flops 1040384 | bytes 6258688 | tf_op jit(solution)/shard_map/stack | solution.py:87
  85.2 2.4 %fusion.39 = (f32[2,1,8,125,256]{4,3,2,1,0:T(8,128)}, f32[2,1,8,125,256]{4,3,2,1,0:T(8,128)}) fusion(f32[1,1,8,128,256]{4,3,2,1,0:T(8,128)S(1)} %bitcast.28, f32[1,1,8,128,256]{4,3,2,1,0:T(8,128)S(1)} %bitcast.40), kind=kLoop, calls=%fused_computation.94 | loop fusion | flops 1024000 | bytes 6193152 | tf_op jit(solution)/shard_map/stack | solution.py:87
  87.7 2.7 %fusion.41 = (f32[2,1,8,128,253]{4,3,2,1,0:T(8,128)}, f32[2,1,8,128,253]{4,3,2,1,0:T(8,128)}) fusion(f32[1,1,8,128,256]{4,3,2,1,0:T(8,128)S(1)} %bitcast.29, f32[1,1,8,128,256]{4,3,2,1,0:T(8,128)S(1)} %bitcast.41), kind=kLoop, calls=%fused_computation.96 | loop fusion | flops 1036288 | bytes 6242304 | tf_op jit(solution)/shard_map/stack | solution.py:87
  92.8 2.6 %fusion.45 = (f32[2,1,8,128,252]{4,3,2,1,0:T(8,128)}, f32[2,1,8,128,252]{4,3,2,1,0:T(8,128)}) fusion(f32[1,1,8,128,256]{4,3,2,1,0:T(8,128)S(1)} %bitcast.31, f32[1,1,8,128,256]{4,3,2,1,0:T(8,128)S(1)} %bitcast.43), kind=kLoop, calls=%fused_computation.100 | loop fusion | flops 1032192 | bytes 6225920 | tf_op jit(solution)/shard_map/stack | solution.py:87
  100.2 11.1 %fusion.61 = f32[2,1,8,128,256]{4,3,2,1,0:T(8,128)S(1)} fusion(f32[2,1,12,128,256]{4,3,2,1,0:T(8,128)S(1)} %get-tuple-element.50, f32[2,1,12,128,256]{4,3,2,1,0:T(8,128)S(1)} %get-tuple-element.49, f32[1,1,8,128,256]{4,3,2,1,0:T(8,128)} %bitcast.49, f32[1,1,8,128,256]{4,3,2,1,0:T(8,128)} %bitcast.50, f32[1,1,8,128,256]{4,3,2,1,0:T(8,128)S(1)} %copy-done.8, ...), kind=kLoop, calls=%fused_computation.119 | loop fusion | flops 19398656 | bytes 59277312 | tf_op jit(solution)/shard_map/add | solution.py:99
  113.0 2.7 %fusion.93 = (f32[2,1,8,128,254]{4,3,2,1,0:T(8,128)}, f32[2,1,8,128,254]{4,3,2,1,0:T(8,128)}) fusion(f32[2,1,8,128,256]{4,3,2,1,0:T(8,128)S(1)} %fusion.61), kind=kLoop, calls=%fused_computation.170 | loop fusion | bytes 8323072 | tf_op jit(solution)/shard_map/slice | solution.py:29
  119.5 5.5 %collective-permute-start.3 = (f32[2,1,4,128,256]{4,3,2,1,0:T(8,128)S(1)}, f32[2,1,4,128,256]{4,3,2,1,0:T(8,128)}, u32[]{:S(2)}, u32[]{:S(2)}) collective-permute-start(f32[2,1,4,128,256]{4,3,2,1,0:T(8,128)S(1)} %get-tuple-element.32), channel_id=1, source_target_pairs={{0,1},{1,2},{2,3},{3,4},{4,5},{5,6},{6,7},{8,9},{9,10},{10,11},{11... | collective-permute-start | bytes 3145736 | tf_op jit(solution)/shard_map/ppermute | solution.py:18
  125.1 2.7 %fusion.95 = (f32[2,1,8,128,253]{4,3,2,1,0:T(8,128)}, f32[2,1,8,128,253]{4,3,2,1,0:T(8,128)}) fusion(f32[2,1,8,128,256]{4,3,2,1,0:T(8,128)S(1)} %fusion.61), kind=kLoop, calls=%fused_computation.172 | loop fusion | bytes 8290304 | tf_op jit(solution)/shard_map/slice | solution.py:29
  127.8 2.4 %fusion.96 = (f32[2,1,8,124,256]{4,3,2,1,0:T(8,128)}, f32[2,1,8,124,256]{4,3,2,1,0:T(8,128)}) fusion(f32[2,1,8,128,256]{4,3,2,1,0:T(8,128)S(1)} %fusion.61), kind=kLoop, calls=%fused_computation.173 | loop fusion | bytes 8126464 | tf_op jit(solution)/shard_map/slice | solution.py:29
  130.2 2.7 %fusion.97 = (f32[2,1,8,128,252]{4,3,2,1,0:T(8,128)}, f32[2,1,8,128,252]{4,3,2,1,0:T(8,128)}) fusion(f32[2,1,8,128,256]{4,3,2,1,0:T(8,128)S(1)} %fusion.61), kind=kLoop, calls=%fused_computation.174 | loop fusion | bytes 8257536 | tf_op jit(solution)/shard_map/slice | solution.py:29
  132.9 11.9 %collective-permute-done.2 = f32[2,1,4,128,256]{4,3,2,1,0:T(8,128)} collective-permute-done((f32[2,1,4,128,256]{4,3,2,1,0:T(8,128)S(1)}, f32[2,1,4,128,256]{4,3,2,1,0:T(8,128)}, u32[]{:S(2)}, u32[]{:S(2)}) %collective-permute-start.2) | collective-permute-done | bytes 1048608 | tf_op jit(solution)/shard_map/ppermute | solution.py:19
  144.9 22.5 %collective-permute-done.3 = f32[2,1,4,128,256]{4,3,2,1,0:T(8,128)} collective-permute-done((f32[2,1,4,128,256]{4,3,2,1,0:T(8,128)S(1)}, f32[2,1,4,128,256]{4,3,2,1,0:T(8,128)}, u32[]{:S(2)}, u32[]{:S(2)}) %collective-permute-start.3) | collective-permute-done | bytes 1048608 | tf_op jit(solution)/shard_map/ppermute | solution.py:18
  167.3 13.1 %fusion.11 = f32[2,1,8,128,256]{4,3,2,1,0:T(8,128)} fusion(f32[2,1,8,128,256]{4,3,2,1,0:T(8,128)S(1)} %fusion.61, f32[2,1,4,128,256]{4,3,2,1,0:T(8,128)} %collective-permute-done.3, f32[2,1,4,128,256]{4,3,2,1,0:T(8,128)} %collective-permute-done.2, f32[1,1,8,128,256]{4,3,2,1,0:T(8,128)S(1)} %copy-done.9, f32[1,1,8,128,256]{4,3,2,1,0:T(8,128)} %stack_reshape.14, ...), kind=kLoop, calls=%fused_computation.66 | loop fusion | flops 23068672 | bytes 44597248 | tf_op jit(solution)/shard_map/add | solution.py:99
  180.4 3.8 %add_bitcast_fusion = (f32[8,128,256]{2,1,0:T(8,128)S(1)}, f32[1,8,128,256]{3,2,1,0:T(8,128)}, f32[1,8,128,256]{3,2,1,0:T(8,128)}, f32[1,8,128,256]{3,2,1,0:T(8,128)}, f32[1,8,128,256]{3,2,1,0:T(8,128)}) fusion(f32[2,1,8,128,256]{4,3,2,1,0:T(8,128)} %fusion.11, f32[2,1,8,128,256]{4,3,2,1,0:T(8,128)S(1)} %fusion.61), kind=kLoop, calls=%fused_computation.146 | loop fusion | flops 786432 | bytes 9437184 | tf_op jit(solution)/shard_map/add | solution.py:104
  187.4 26.4 %reduce-scatter.2.cloned.1.call-done = f32[8,32,256]{2,1,0:T(8,128)} async-done(((f32[8,128,256]{2,1,0:T(8,128)}), f32[8,32,256]{2,1,0:T(8,128)}) %reduce-scatter.2.cloned.1.call-update) | async-done | bytes 262160 | tf_op jit(solution)/shard_map/reduce_scatter | solution.py:107
  214.9 14.2 %all_to_all.18 = f32[8,32,256]{2,0,1:T(8,128)S(1)} all-to-all(f32[8,32,256]{2,0,1:T(8,128)S(1)} %copy.28), channel_id=1, replica_groups=mesh['shots'=4,'depth'=8] {'depth'}, dimensions={1} | all-to-all | bytes 524288 | tf_op jit(solution)/shard_map/all_to_all | solution.py:108
  (67 shorter events, 26.9 us)
Async XLA Ops:
  7.2 206.6 %reduce-scatter.2.cloned.1.call-start = ((), (), s32[]{:S(2)}) async-start(), calls=%async_computation.2 | async-start | bytes 1310720 | tf_op jit(solution)/shard_map/reduce_scatter | solution.py:107
  7.2 11.0 %copy-start = (f32[1,8,128,256]{3,2,1,0:T(8,128)S(1)}, f32[1,8,128,256]{3,2,1,0:T(8,128)}, u32[]{:S(2)}) copy-start(f32[1,8,128,256]{3,2,1,0:T(8,128)} %param.13) | copy-start | bytes 3145732
  7.2 11.0 %copy-start.1 = (f32[1,8,128,256]{3,2,1,0:T(8,128)S(1)}, f32[1,8,128,256]{3,2,1,0:T(8,128)}, u32[]{:S(2)}) copy-start(f32[1,8,128,256]{3,2,1,0:T(8,128)} %param.15) | copy-start | bytes 3145732
  10.4 85.1 %collective-permute-start = (f32[2,1,4,128,256]{4,3,2,1,0:T(8,128)}, f32[2,1,4,128,256]{4,3,2,1,0:T(8,128)}, u32[]{:S(2)}, u32[]{:S(2)}) collective-permute-start(f32[2,1,4,128,256]{4,3,2,1,0:T(8,128)} %get-tuple-element.51), channel_id=1, source_target_pairs={{1,0},{2,1},{3,2},{4,3},{5,4},{6,5},{7,6},{9,8},{10,9},{11,10},{12... | collective-permute-start | bytes 3145736 | tf_op jit(solution)/shard_map/ppermute | solution.py:19
  11.7 83.8 %collective-permute-start.1 = (f32[2,1,4,128,256]{4,3,2,1,0:T(8,128)}, f32[2,1,4,128,256]{4,3,2,1,0:T(8,128)}, u32[]{:S(2)}, u32[]{:S(2)}) collective-permute-start(f32[2,1,4,128,256]{4,3,2,1,0:T(8,128)} %get-tuple-element.52), channel_id=1, source_target_pairs={{0,1},{1,2},{2,3},{3,4},{4,5},{5,6},{6,7},{8,9},{9,10},{10,11},{11... | collective-permute-start | bytes 3145736 | tf_op jit(solution)/shard_map/ppermute | solution.py:18
  23.4 2.4 %copy-start.10 = (f32[1,2,4096]{2,1,0:T(2,128)S(1)}, f32[1,2,4096]{2,1,0:T(2,128)}, u32[]{:S(2)}) copy-start(f32[1,2,4096]{2,1,0:T(2,128)} %param.23) | copy-start | bytes 98308
  23.4 2.5 %copy-start.11 = (s32[4096]{0:T(1024)S(1)}, s32[4096]{0:T(1024)}, u32[]{:S(2)}) copy-start(s32[4096]{0:T(1024)} %param.22) | copy-start | bytes 49156
  23.4 2.5 %copy-start.12 = (s32[4096]{0:T(1024)S(1)}, s32[4096]{0:T(1024)}, u32[]{:S(2)}) copy-start(s32[4096]{0:T(1024)} %param.21) | copy-start | bytes 49156
  25.8 23.5 %copy-start.15 = (s32[512]{0:T(512)S(1)}, s32[512]{0:T(512)}, u32[]{:S(2)}) copy-start(s32[512]{0:T(512)} %param.20) | copy-start | bytes 6148
  25.8 23.5 %copy-start.16 = (s32[512]{0:T(512)S(1)}, s32[512]{0:T(512)}, u32[]{:S(2)}) copy-start(s32[512]{0:T(512)} %param.19) | copy-start | bytes 6148
  25.8 23.6 %copy-start.13 = (f32[2,512]{1,0:T(2,128)S(1)}, f32[2,512]{1,0:T(2,128)}, u32[]{:S(2)}) copy-start(f32[2,512]{1,0:T(2,128)} %param.17) | copy-start | bytes 12292
  25.8 23.6 %copy-start.14 = (s32[1,512]{1,0:T(1,128)S(1)}, s32[1,512]{1,0:T(1,128)}, u32[]{:S(2)}) copy-start(s32[1,512]{1,0:T(1,128)} %param.18) | copy-start | bytes 6148
  92.8 4.9 %copy-start.7 = (f32[8,128,256]{2,1,0:T(8,128)S(1)}, f32[8,128,256]{2,1,0:T(8,128)}, u32[]{:S(2)}) copy-start(f32[8,128,256]{2,1,0:T(8,128)} %param.16) | copy-start | bytes 3145732
  92.8 4.9 %copy-start.8 = (f32[1,1,8,128,256]{4,3,2,1,0:T(8,128)S(1)}, f32[1,1,8,128,256]{4,3,2,1,0:T(8,128)}, u32[]{:S(2)}) copy-start(f32[1,1,8,128,256]{4,3,2,1,0:T(8,128)} %stack_reshape.13) | copy-start | bytes 3145732
  95.5 2.3 copy-start.2
  95.5 2.9 %copy-start.3 = (f32[2,1,8,127,256]{4,3,2,1,0:T(8,128)S(1)}, f32[2,1,8,127,256]{4,3,2,1,0:T(8,128)}, u32[]{:S(2)}) copy-start(f32[2,1,8,127,256]{4,3,2,1,0:T(8,128)} %get-tuple-element.34) | copy-start | bytes 6242308
  95.5 3.5 %copy-start.4 = (f32[2,1,8,128,255]{4,3,2,1,0:T(8,128)S(1)}, f32[2,1,8,128,255]{4,3,2,1,0:T(8,128)}, u32[]{:S(2)}) copy-start(f32[2,1,8,128,255]{4,3,2,1,0:T(8,128)} %get-tuple-element.35) | copy-start | bytes 6266884
  95.5 4.1 %copy-start.5 = (f32[2,1,8,128,255]{4,3,2,1,0:T(8,128)S(1)}, f32[2,1,8,128,255]{4,3,2,1,0:T(8,128)}, u32[]{:S(2)}) copy-start(f32[2,1,8,128,255]{4,3,2,1,0:T(8,128)} %get-tuple-element.36) | copy-start | bytes 6266884
  95.5 4.7 %copy-start.6 = (f32[2,1,8,126,256]{4,3,2,1,0:T(8,128)S(1)}, f32[2,1,8,126,256]{4,3,2,1,0:T(8,128)}, u32[]{:S(2)}) copy-start(f32[2,1,8,126,256]{4,3,2,1,0:T(8,128)} %get-tuple-element.37) | copy-start | bytes 6193156
  118.2 26.6 %collective-permute-start.2 = (f32[2,1,4,128,256]{4,3,2,1,0:T(8,128)S(1)}, f32[2,1,4,128,256]{4,3,2,1,0:T(8,128)}, u32[]{:S(2)}, u32[]{:S(2)}) collective-permute-start(f32[2,1,4,128,256]{4,3,2,1,0:T(8,128)S(1)} %get-tuple-element.31), channel_id=1, source_target_pairs={{1,0},{2,1},{3,2},{4,3},{5,4},{6,5},{7,6},{9,8},{10,9},{11,10},{12... | collective-permute-start | bytes 3145736 | tf_op jit(solution)/shard_map/ppermute | solution.py:19
  119.5 47.8 %collective-permute-start.3 = (f32[2,1,4,128,256]{4,3,2,1,0:T(8,128)S(1)}, f32[2,1,4,128,256]{4,3,2,1,0:T(8,128)}, u32[]{:S(2)}, u32[]{:S(2)}) collective-permute-start(f32[2,1,4,128,256]{4,3,2,1,0:T(8,128)S(1)} %get-tuple-element.32), channel_id=1, source_target_pairs={{0,1},{1,2},{2,3},{3,4},{4,5},{5,6},{6,7},{8,9},{9,10},{10,11},{11... | collective-permute-start | bytes 3145736 | tf_op jit(solution)/shard_map/ppermute | solution.py:18
  130.2 37.1 %copy-start.9 = (f32[1,1,8,128,256]{4,3,2,1,0:T(8,128)S(1)}, f32[1,1,8,128,256]{4,3,2,1,0:T(8,128)}, u32[]{:S(2)}) copy-start(f32[1,1,8,128,256]{4,3,2,1,0:T(8,128)} %stack_reshape.15) | copy-start | bytes 3145732
Sparse Core Ops, SparseCore 0:
  187.5 26.1 reduce-scatter.1
where the time goes:
time: 237 us
  other arithmetic  108 us (46%)
  waiting for transfers between devices  60.8 us (26%)
  local copies, waits for them, and re-layouts  24.8 us (10%)
  starting transfers between devices  14.6 us (6%)
  between operations  14.3 us (6%)
  blocking collectives  14.2 us (6%)
    scatter-add x4, other arithmetic, spread(): jnp.zeros((values.shape[0], limit), jnp.float32).at[:, local]  51.5 us
    reduce_scatter x1, waiting for transfers between devices, on_device(): lax.psum_scatter(lateral_smooth, 'shots', scatter_dimension=1, tiled=True)  26.4 us
    add x2, other arithmetic, on_device(): 2.0 * current - earlier + courant * laplace(extended)  24.2 us
    another operation x9, other arithmetic, on_device(): current = jnp.stack([forward_now, adjoint_now])  23.7 us
    ppermute x2, waiting for transfers between devices, extended_2(): before = lax.ppermute(last, axis, up)  22.5 us
    slice x14, local copies, waits for them, and re-layouts, shifted(): kept = lax.slice_in_dim(values, offset, size, axis=axis)  15.8 us
    all_to_all x1, blocking collectives, on_device(): lax.all_to_all(summed, 'depth', split_axis=1, concat_axis=0, tiled=True)  14.2 us
    ppermute x2, starting transfers between devices, extended_2(): before = lax.ppermute(last, axis, up)  12 us
  transfers between devices with their start and end apart: 5, of which 3 were waited for; matrix products, arithmetic and copies ran while one was open for 36% of the time, Pallas kernels for 0%

commit v1 on v0

--- a/solution.py
+++ b/solution.py
@@ -6,6 +6,29 @@
 STEPS = 2
 COEFFS = (-205.0 / 72.0, 8.0 / 5.0, -1.0 / 5.0, 8.0 / 315.0, -1.0 / 560.0)
 KERNEL = (1.0 / 16.0, 4.0 / 16.0, 6.0 / 16.0, 4.0 / 16.0, 1.0 / 16.0)
+
+
+def cut_along(value, dim, size):
+    before, after = (value.shape[:dim], value.shape[dim + 1 :])
+    return jnp.moveaxis(value.reshape(*before, size, -1, *after), dim, 0)
+
+
+def joined_along(blocks, dim):
+    shape = list(blocks.shape[1:])
+    shape[dim] *= blocks.shape[0]
+    return jnp.moveaxis(blocks, 0, dim).reshape(shape)
+
+
+def sent_to_each(x, axis, split_dim, concat_dim):
+    size, mine = (lax.axis_size(axis), lax.axis_index(axis))
+    tiles = cut_along(x, split_dim, size)
+    out = tiles
+    for step in range(1, size):
+        target, source = ((mine + step) % size, (mine - step) % size)
+        sent = lax.dynamic_index_in_dim(tiles, target, 0)
+        theirs = lax.ppermute(sent, axis, [(i, (i + step) % size) for i in range(size)])
+        out = lax.dynamic_update_slice_in_dim(out, theirs, source, axis=0)
+    return joined_along(out, concat_dim)
 
 
 def extended_2(shard, sides, width):
@@ -105,7 +128,7 @@
         earlier, current = (current, fresh)
     lateral_smooth = smooth(smooth(correlation, 1), 2)
     summed = lax.psum_scatter(lateral_smooth, "shots", scatter_dimension=1, tiled=True)
-    columns = lax.all_to_all(summed, "depth", split_axis=1, concat_axis=0, tiled=True)
+    columns = sent_to_each(summed, "depth", 1, 0)
     gradient = smooth(columns, 0)
     return (earlier[0], current[0], earlier[1], current[1], gradient)
 

time: 237 us -> 245 us (1.034)
  blocking collectives: 14.2 us -> 0 us
  starting transfers between devices: 14.6 us -> 26.9 us
  other arithmetic: 108 us -> 112 us
  local copies, waits for them, and re-layouts: 24.8 us -> 28.4 us
    all_to_all x1 -> x0, blocking collectives: 14.2 us -> none  [on_device(): lax.all_to_all(summed, 'depth', split_axis=1, concat_axis=0, tiled=True)]
    ppermute x0 -> x7, starting transfers between devices: none -> 12.3 us  [sent_to_each(): lax.ppermute(sent, axis, [(i, (i + step) % size) for i in range(size)])]
    another operation x4, local copies, waits for them, and re-layouts: 5.06 us -> 9.03 us  [on_device(): jnp.stack([forward_part, adjoint_part])]
    scatter-add x4, other arithmetic: 51.5 us -> 54.3 us  [spread(): jnp.zeros((values.shape[0], limit), jnp.float32).at[:, local]]
  transfers between devices with their start and end apart: 5 -> 12, of which waited for: 3 -> 5; matrix products, arithmetic and copies ran while one was open for 36% -> 38% of each run, Pallas kernels for 0% -> 0%
where the time goes in v1:
time: 245 us; the launch traced here: 244 us
  other arithmetic  112 us (46%)
  waiting for transfers between devices  63 us (26%)
  local copies, waits for them, and re-layouts  28.4 us (12%)
  starting transfers between devices  26.9 us (11%)
  between operations  14.5 us (6%)
    scatter-add x4, other arithmetic, spread(): jnp.zeros((values.shape[0], limit), jnp.float32).at[:, local]  54.3 us
    reduce_scatter x1, waiting for transfers between devices, on_device(): lax.psum_scatter(lateral_smooth, 'shots', scatter_dimension=1, tiled=True)  26.2 us
    add x2, other arithmetic, on_device(): 2.0 * current - earlier + courant * laplace(extended)  24.3 us
    another operation x9, other arithmetic, on_device(): current = jnp.stack([forward_now, adjoint_now])  23.7 us
    ppermute x2, waiting for transfers between devices, extended_2(): before = lax.ppermute(last, axis, up)  22.5 us
    slice x14, local copies, waits for them, and re-layouts, shifted(): kept = lax.slice_in_dim(values, offset, size, axis=axis)  15.8 us
    ppermute x7, starting transfers between devices, sent_to_each(): lax.ppermute(sent, axis, [(i, (i + step) % size) for i in range(size)])  12.3 us
    ppermute x2, starting transfers between devices, extended_2(): before = lax.ppermute(last, axis, up)  12 us
  transfers between devices with their start and end apart: 12, of which 5 were waited for; matrix products, arithmetic and copies ran while one was open for 38% of the time, Pallas kernels for 0%

profile of v1, /device:TPU:0, one launch (start us, length us, event | category | flops | bytes accessed | tf_op | source)
XLA Modules:
  0.0 244.3 jit_solution(8780602163311654023)
XLA Ops:
  7.2 3.2 %fusion.80 = (f32[2,1,4,128,256]{4,3,2,1,0:T(8,128)}, f32[2,1,4,128,256]{4,3,2,1,0:T(8,128)}) fusion(f32[1,1,8,128,256]{4,3,2,1,0:T(8,128)} %bitcast.37, f32[1,1,8,128,256]{4,3,2,1,0:T(8,128)} %bitcast.49), kind=kLoop, calls=%fused_computation.142 | loop fusion | flops 524288 | bytes 4194304 | tf_op jit(solution)/shard_map/stack | solution.py:110
  11.7 6.5 %collective-permute-start.1 = (f32[2,1,4,128,256]{4,3,2,1,0:T(8,128)}, f32[2,1,4,128,256]{4,3,2,1,0:T(8,128)}, u32[]{:S(2)}, u32[]{:S(2)}) collective-permute-start(f32[2,1,4,128,256]{4,3,2,1,0:T(8,128)} %get-tuple-element.47), channel_id=1, source_target_pairs={{0,1},{1,2},{2,3},{3,4},{4,5},{5,6},{6,7},{8,9},{9,10},{10,11},{11... | collective-permute-start | bytes 3145736 | tf_op jit(solution)/shard_map/ppermute | solution.py:41
  20.6 2.7 %fusion.33 = (f32[2,1,8,128,255]{4,3,2,1,0:T(8,128)}, f32[2,1,8,128,255]{4,3,2,1,0:T(8,128)}) fusion(f32[1,1,8,128,256]{4,3,2,1,0:T(8,128)S(1)} %bitcast.39, f32[1,1,8,128,256]{4,3,2,1,0:T(8,128)S(1)} %bitcast.51), kind=kLoop, calls=%fused_computation.88 | loop fusion | flops 1044480 | bytes 6275072 | tf_op jit(solution)/shard_map/stack | solution.py:110
  25.9 22.9 %scatter_custom_fusion.1 = f32[262144]{0:T(1024)} fusion(s32[4096]{0:T(1024)S(1)} %compare_select_fusion, f32[4096]{0:T(1024)S(1)} %bitcast.67, f32[]{:T(128)} %constant.138.clone.1), kind=kCustom, calls=%fused_computation.155 | custom fusion | flops 4096 | bytes 1048580 | tf_op jit(solution)/shard_map/scatter-add | solution.py:85
  50.4 4.3 %scatter_custom_fusion = f32[262144]{0:T(1024)} fusion(s32[512]{0:T(512)S(1)} %compare_select_fusion.1, f32[512]{0:T(512)S(1)} %bitcast.69, f32[]{:T(128)} %constant.138.clone.1), kind=kCustom, calls=%fused_computation.157 | custom fusion | flops 512 | bytes 1048580 | tf_op jit(solution)/shard_map/scatter-add | solution.py:85
  54.7 2.5 %stack_reshape.12 = f32[1,1,8,128,256]{4,3,2,1,0:T(8,128)} reshape(f32[262144]{0:T(1024)} %scatter_custom_fusion) | data formatting | bytes 2097152 | tf_op jit(solution)/shard_map/stack;reshape | solution.py:125
  57.1 22.9 %scatter_custom_fusion.3 = f32[262144]{0:T(1024)} fusion(s32[4096]{0:T(1024)S(1)} %compare_select_fusion, f32[4096]{0:T(1024)S(1)} %bitcast.66, f32[]{:T(128)} %constant.138.clone.1), kind=kCustom, calls=%fused_computation.151 | custom fusion | flops 4096 | bytes 1048580 | tf_op jit(solution)/shard_map/scatter-add | solution.py:85
  80.0 2.5 %stack_reshape.15 = f32[1,1,8,128,256]{4,3,2,1,0:T(8,128)} reshape(f32[262144]{0:T(1024)} %scatter_custom_fusion.3) | data formatting | bytes 2097152 | tf_op jit(solution)/shard_map/stack;reshape | solution.py:125
  82.5 4.2 %scatter_custom_fusion.2 = f32[262144]{0:T(1024)} fusion(s32[512]{0:T(512)S(1)} %compare_select_fusion.1, f32[512]{0:T(512)S(1)} %bitcast.68, f32[]{:T(128)} %constant.138.clone.1), kind=kCustom, calls=%fused_computation.153 | custom fusion | flops 512 | bytes 1048580 | tf_op jit(solution)/shard_map/scatter-add | solution.py:85
  86.8 2.5 %stack_reshape.14 = f32[1,1,8,128,256]{4,3,2,1,0:T(8,128)} reshape(f32[262144]{0:T(1024)} %scatter_custom_fusion.2) | data formatting | bytes 2097152 | tf_op jit(solution)/shard_map/stack;reshape | solution.py:125
  89.3 2.7 %fusion.37 = (f32[2,1,8,128,254]{4,3,2,1,0:T(8,128)}, f32[2,1,8,128,254]{4,3,2,1,0:T(8,128)}) fusion(f32[1,1,8,128,256]{4,3,2,1,0:T(8,128)S(1)} %bitcast.41, f32[1,1,8,128,256]{4,3,2,1,0:T(8,128)S(1)} %bitcast.53), kind=kLoop, calls=%fused_computation.92 | loop fusion | flops 1040384 | bytes 6258688 | tf_op jit(solution)/shard_map/stack | solution.py:110
  94.4 2.7 %fusion.41 = (f32[2,1,8,128,253]{4,3,2,1,0:T(8,128)}, f32[2,1,8,128,253]{4,3,2,1,0:T(8,128)}) fusion(f32[1,1,8,128,256]{4,3,2,1,0:T(8,128)S(1)} %bitcast.43, f32[1,1,8,128,256]{4,3,2,1,0:T(8,128)S(1)} %bitcast.55), kind=kLoop, calls=%fused_computation.96 | loop fusion | flops 1036288 | bytes 6242304 | tf_op jit(solution)/shard_map/stack | solution.py:110
  99.6 2.6 %fusion.45 = (f32[2,1,8,128,252]{4,3,2,1,0:T(8,128)}, f32[2,1,8,128,252]{4,3,2,1,0:T(8,128)}) fusion(f32[1,1,8,128,256]{4,3,2,1,0:T(8,128)S(1)} %bitcast.45, f32[1,1,8,128,256]{4,3,2,1,0:T(8,128)S(1)} %bitcast.57), kind=kLoop, calls=%fused_computation.100 | loop fusion | flops 1032192 | bytes 6225920 | tf_op jit(solution)/shard_map/stack | solution.py:110
  102.2 2.5 %pad_maximum_fusion.1 = (f32[2,1,12,128,256]{4,3,2,1,0:T(8,128)S(1)}, f32[2,1,12,128,256]{4,3,2,1,0:T(8,128)S(1)}) fusion(f32[2,1,4,128,256]{4,3,2,1,0:T(8,128)} %collective-permute-done, f32[1,1,8,128,256]{4,3,2,1,0:T(8,128)S(1)} %bitcast.58, f32[1,1,8,128,256]{4,3,2,1,0:T(8,128)S(1)} %bitcast.46, f32[2,1,4,128,256]{4,3,2,1,0:T(8,128)} %collective-permute-done.1), kind=kLoop, calls=%fused_computation.53 | loop fusion | flops 3145728 | bytes 10485760 | tf_op jit(solution)/shard_map/concatenate | solution.py:43
  106.9 11.1 %fusion.61 = f32[2,1,8,128,256]{4,3,2,1,0:T(8,128)S(1)} fusion(f32[2,1,12,128,256]{4,3,2,1,0:T(8,128)S(1)} %get-tuple-element.45, f32[2,1,12,128,256]{4,3,2,1,0:T(8,128)S(1)} %get-tuple-element.44, f32[1,1,8,128,256]{4,3,2,1,0:T(8,128)} %bitcast.64, f32[1,1,8,128,256]{4,3,2,1,0:T(8,128)} %bitcast.65, f32[1,1,8,128,256]{4,3,2,1,0:T(8,128)S(1)} %stack_reshape.13, ...), kind=kLoop, calls=%fused_computation.119 | loop fusion | flops 19398656 | bytes 59277312 | tf_op jit(solution)/shard_map/add | solution.py:122
  119.8 2.7 %fusion.93 = (f32[2,1,8,128,254]{4,3,2,1,0:T(8,128)}, f32[2,1,8,128,254]{4,3,2,1,0:T(8,128)}) fusion(f32[2,1,8,128,256]{4,3,2,1,0:T(8,128)S(1)} %fusion.61), kind=kLoop, calls=%fused_computation.185 | loop fusion | bytes 8323072 | tf_op jit(solution)/shard_map/slice | solution.py:52
  126.3 5.5 %collective-permute-start.3 = (f32[2,1,4,128,256]{4,3,2,1,0:T(8,128)S(1)}, f32[2,1,4,128,256]{4,3,2,1,0:T(8,128)}, u32[]{:S(2)}, u32[]{:S(2)}) collective-permute-start(f32[2,1,4,128,256]{4,3,2,1,0:T(8,128)S(1)} %get-tuple-element.27), channel_id=1, source_target_pairs={{0,1},{1,2},{2,3},{3,4},{4,5},{5,6},{6,7},{8,9},{9,10},{10,11},{11... | collective-permute-start | bytes 3145736 | tf_op jit(solution)/shard_map/ppermute | solution.py:41
  131.9 2.8 %fusion.95 = (f32[2,1,8,128,253]{4,3,2,1,0:T(8,128)}, f32[2,1,8,128,253]{4,3,2,1,0:T(8,128)}) fusion(f32[2,1,8,128,256]{4,3,2,1,0:T(8,128)S(1)} %fusion.61), kind=kLoop, calls=%fused_computation.187 | loop fusion | bytes 8290304 | tf_op jit(solution)/shard_map/slice | solution.py:52
  137.0 2.7 %fusion.97 = (f32[2,1,8,128,252]{4,3,2,1,0:T(8,128)}, f32[2,1,8,128,252]{4,3,2,1,0:T(8,128)}) fusion(f32[2,1,8,128,256]{4,3,2,1,0:T(8,128)S(1)} %fusion.61), kind=kLoop, calls=%fused_computation.189 | loop fusion | bytes 8257536 | tf_op jit(solution)/shard_map/slice | solution.py:52
  139.7 11.9 %collective-permute-done.2 = f32[2,1,4,128,256]{4,3,2,1,0:T(8,128)} collective-permute-done((f32[2,1,4,128,256]{4,3,2,1,0:T(8,128)S(1)}, f32[2,1,4,128,256]{4,3,2,1,0:T(8,128)}, u32[]{:S(2)}, u32[]{:S(2)}) %collective-permute-start.2) | collective-permute-done | bytes 1048608 | tf_op jit(solution)/shard_map/ppermute | solution.py:42
  151.6 22.5 %collective-permute-done.3 = f32[2,1,4,128,256]{4,3,2,1,0:T(8,128)} collective-permute-done((f32[2,1,4,128,256]{4,3,2,1,0:T(8,128)S(1)}, f32[2,1,4,128,256]{4,3,2,1,0:T(8,128)}, u32[]{:S(2)}, u32[]{:S(2)}) %collective-permute-start.3) | collective-permute-done | bytes 1048608 | tf_op jit(solution)/shard_map/ppermute | solution.py:41
  174.1 13.1 %fusion.11 = f32[2,1,8,128,256]{4,3,2,1,0:T(8,128)} fusion(f32[2,1,8,128,256]{4,3,2,1,0:T(8,128)S(1)} %fusion.61, f32[2,1,4,128,256]{4,3,2,1,0:T(8,128)} %collective-permute-done.3, f32[2,1,4,128,256]{4,3,2,1,0:T(8,128)} %collective-permute-done.2, f32[1,1,8,128,256]{4,3,2,1,0:T(8,128)S(1)} %copy-done.8, f32[1,1,8,128,256]{4,3,2,1,0:T(8,128)} %stack_reshape.14, ...), kind=kLoop, calls=%fused_computation.66 | loop fusion | flops 23068672 | bytes 44597248 | tf_op jit(solution)/shard_map/add | solution.py:122
  187.2 3.8 %add_bitcast_fusion = (f32[8,128,256]{2,1,0:T(8,128)S(1)}, f32[1,8,128,256]{3,2,1,0:T(8,128)}, f32[1,8,128,256]{3,2,1,0:T(8,128)}, f32[1,8,128,256]{3,2,1,0:T(8,128)}, f32[1,8,128,256]{3,2,1,0:T(8,128)}) fusion(f32[2,1,8,128,256]{4,3,2,1,0:T(8,128)} %fusion.11, f32[2,1,8,128,256]{4,3,2,1,0:T(8,128)S(1)} %fusion.61), kind=kLoop, calls=%fused_computation.146 | loop fusion | flops 786432 | bytes 9437184 | tf_op jit(solution)/shard_map/add | solution.py:127
  194.3 26.2 %reduce-scatter.2.cloned.1.call-done = f32[8,32,256]{2,1,0:T(8,128)} async-done(((f32[8,128,256]{2,1,0:T(8,128)}), f32[8,32,256]{2,1,0:T(8,128)}) %reduce-scatter.2.cloned.1.call-update) | async-done | bytes 262160 | tf_op jit(solution)/shard_map/reduce_scatter | solution.py:130
  (86 shorter events, 42.8 us)
Async XLA Ops:
  7.2 213.4 %reduce-scatter.2.cloned.1.call-start = ((), (), s32[]{:S(2)}) async-start(), calls=%async_computation.1 | async-start | bytes 1310720 | tf_op jit(solution)/shard_map/reduce_scatter | solution.py:130
  7.2 11.0 %copy-start = (f32[1,8,128,256]{3,2,1,0:T(8,128)S(1)}, f32[1,8,128,256]{3,2,1,0:T(8,128)}, u32[]{:S(2)}) copy-start(f32[1,8,128,256]{3,2,1,0:T(8,128)} %param.13) | copy-start | bytes 3145732
  7.2 11.0 %copy-start.1 = (f32[1,8,128,256]{3,2,1,0:T(8,128)S(1)}, f32[1,8,128,256]{3,2,1,0:T(8,128)}, u32[]{:S(2)}) copy-start(f32[1,8,128,256]{3,2,1,0:T(8,128)} %param.15) | copy-start | bytes 3145732
  10.4 91.8 %collective-permute-start = (f32[2,1,4,128,256]{4,3,2,1,0:T(8,128)}, f32[2,1,4,128,256]{4,3,2,1,0:T(8,128)}, u32[]{:S(2)}, u32[]{:S(2)}) collective-permute-start(f32[2,1,4,128,256]{4,3,2,1,0:T(8,128)} %get-tuple-element.46), channel_id=1, source_target_pairs={{1,0},{2,1},{3,2},{4,3},{5,4},{6,5},{7,6},{9,8},{10,9},{11,10},{12... | collective-permute-start | bytes 3145736 | tf_op jit(solution)/shard_map/ppermute | solution.py:42
  11.7 90.6 %collective-permute-start.1 = (f32[2,1,4,128,256]{4,3,2,1,0:T(8,128)}, f32[2,1,4,128,256]{4,3,2,1,0:T(8,128)}, u32[]{:S(2)}, u32[]{:S(2)}) collective-permute-start(f32[2,1,4,128,256]{4,3,2,1,0:T(8,128)} %get-tuple-element.47), channel_id=1, source_target_pairs={{0,1},{1,2},{2,3},{3,4},{4,5},{5,6},{6,7},{8,9},{9,10},{10,11},{11... | collective-permute-start | bytes 3145736 | tf_op jit(solution)/shard_map/ppermute | solution.py:41
  25.8 24.5 %copy-start.14 = (s32[512]{0:T(512)S(1)}, s32[512]{0:T(512)}, u32[]{:S(2)}) copy-start(s32[512]{0:T(512)} %param.20) | copy-start | bytes 6148
  25.8 24.6 %copy-start.15 = (s32[512]{0:T(512)S(1)}, s32[512]{0:T(512)}, u32[]{:S(2)}) copy-start(s32[512]{0:T(512)} %param.19) | copy-start | bytes 6148
  25.8 24.6 %copy-start.12 = (f32[2,512]{1,0:T(2,128)S(1)}, f32[2,512]{1,0:T(2,128)}, u32[]{:S(2)}) copy-start(f32[2,512]{1,0:T(2,128)} %param.17) | copy-start | bytes 12292
  25.8 24.6 %copy-start.13 = (s32[1,512]{1,0:T(1,128)S(1)}, s32[1,512]{1,0:T(1,128)}, u32[]{:S(2)}) copy-start(s32[1,512]{1,0:T(1,128)} %param.18) | copy-start | bytes 6148
  99.6 5.2 %copy-start.7 = (f32[8,128,256]{2,1,0:T(8,128)S(1)}, f32[8,128,256]{2,1,0:T(8,128)}, u32[]{:S(2)}) copy-start(f32[8,128,256]{2,1,0:T(8,128)} %param.16) | copy-start | bytes 3145732
  102.2 2.9 %copy-start.3 = (f32[2,1,8,127,256]{4,3,2,1,0:T(8,128)S(1)}, f32[2,1,8,127,256]{4,3,2,1,0:T(8,128)}, u32[]{:S(2)}) copy-start(f32[2,1,8,127,256]{4,3,2,1,0:T(8,128)} %get-tuple-element.29) | copy-start | bytes 6242308
  102.2 3.5 %copy-start.4 = (f32[2,1,8,128,255]{4,3,2,1,0:T(8,128)S(1)}, f32[2,1,8,128,255]{4,3,2,1,0:T(8,128)}, u32[]{:S(2)}) copy-start(f32[2,1,8,128,255]{4,3,2,1,0:T(8,128)} %get-tuple-element.30) | copy-start | bytes 6266884
  102.2 4.1 %copy-start.5 = (f32[2,1,8,128,255]{4,3,2,1,0:T(8,128)S(1)}, f32[2,1,8,128,255]{4,3,2,1,0:T(8,128)}, u32[]{:S(2)}) copy-start(f32[2,1,8,128,255]{4,3,2,1,0:T(8,128)} %get-tuple-element.31) | copy-start | bytes 6266884
  102.2 4.7 %copy-start.6 = (f32[2,1,8,126,256]{4,3,2,1,0:T(8,128)S(1)}, f32[2,1,8,126,256]{4,3,2,1,0:T(8,128)}, u32[]{:S(2)}) copy-start(f32[2,1,8,126,256]{4,3,2,1,0:T(8,128)} %get-tuple-element.32) | copy-start | bytes 6193156
  125.0 26.6 %collective-permute-start.2 = (f32[2,1,4,128,256]{4,3,2,1,0:T(8,128)S(1)}, f32[2,1,4,128,256]{4,3,2,1,0:T(8,128)}, u32[]{:S(2)}, u32[]{:S(2)}) collective-permute-start(f32[2,1,4,128,256]{4,3,2,1,0:T(8,128)S(1)} %get-tuple-element.26), channel_id=1, source_target_pairs={{1,0},{2,1},{3,2},{4,3},{5,4},{6,5},{7,6},{9,8},{10,9},{11,10},{12... | collective-permute-start | bytes 3145736 | tf_op jit(solution)/shard_map/ppermute | solution.py:42
  126.3 47.8 %collective-permute-start.3 = (f32[2,1,4,128,256]{4,3,2,1,0:T(8,128)S(1)}, f32[2,1,4,128,256]{4,3,2,1,0:T(8,128)}, u32[]{:S(2)}, u32[]{:S(2)}) collective-permute-start(f32[2,1,4,128,256]{4,3,2,1,0:T(8,128)S(1)} %get-tuple-element.27), channel_id=1, source_target_pairs={{0,1},{1,2},{2,3},{3,4},{4,5},{5,6},{6,7},{8,9},{9,10},{10,11},{11... | collective-permute-start | bytes 3145736 | tf_op jit(solution)/shard_map/ppermute | solution.py:41
  137.0 37.1 %copy-start.8 = (f32[1,1,8,128,256]{4,3,2,1,0:T(8,128)S(1)}, f32[1,1,8,128,256]{4,3,2,1,0:T(8,128)}, u32[]{:S(2)}) copy-start(f32[1,1,8,128,256]{4,3,2,1,0:T(8,128)} %stack_reshape.15) | copy-start | bytes 3145732
  221.6 9.3 %collective-permute-start.4 = (f32[1,8,4,256]{3,2,1,0:T(4,128)S(1)}, f32[1,8,4,256]{3,2,1,0:T(4,128)S(1)}, u32[]{:S(2)}, u32[]{:S(2)}) collective-permute-start(f32[1,8,4,256]{3,2,1,0:T(4,128)S(1)} %get-tuple-element.66), channel_id=1, source_target_pairs={{0,1},{1,2},{2,3},{3,4},{4,5},{5,6},{6,7},{7,0},{8,9},{9,10},{10,1... | collective-permute-start | bytes 98312 | tf_op jit(solution)/shard_map/ppermute | solution.py:29
  223.2 9.2 %collective-permute-start.5 = (f32[1,8,4,256]{3,2,1,0:T(4,128)S(1)}, f32[1,8,4,256]{3,2,1,0:T(4,128)S(1)}, u32[]{:S(2)}, u32[]{:S(2)}) collective-permute-start(f32[1,8,4,256]{3,2,1,0:T(4,128)S(1)} %get-tuple-element.65), channel_id=1, source_target_pairs={{0,2},{1,3},{2,4},{3,5},{4,6},{5,7},{6,0},{7,1},{8,10},{9,11},{10,... | collective-permute-start | bytes 98312 | tf_op jit(solution)/shard_map/ppermute | solution.py:29
  224.7 9.2 %collective-permute-start.6 = (f32[1,8,4,256]{3,2,1,0:T(4,128)S(1)}, f32[1,8,4,256]{3,2,1,0:T(4,128)S(1)}, u32[]{:S(2)}, u32[]{:S(2)}) collective-permute-start(f32[1,8,4,256]{3,2,1,0:T(4,128)S(1)} %get-tuple-element.64), channel_id=1, source_target_pairs={{0,3},{1,4},{2,5},{3,6},{4,7},{5,0},{6,1},{7,2},{8,11},{9,12},{10,... | collective-permute-start | bytes 98312 | tf_op jit(solution)/shard_map/ppermute | solution.py:29
  227.1 6.8 %collective-permute-start.7 = (f32[1,8,4,256]{3,2,1,0:T(4,128)S(1)}, f32[1,8,4,256]{3,2,1,0:T(4,128)S(1)}, u32[]{:S(2)}, u32[]{:S(2)}) collective-permute-start(f32[1,8,4,256]{3,2,1,0:T(4,128)S(1)} %get-tuple-element.63), channel_id=1, source_target_pairs={{0,4},{1,5},{2,6},{3,7},{4,0},{5,1},{6,2},{7,3},{8,12},{9,13},{10,... | collective-permute-start | bytes 98312 | tf_op jit(solution)/shard_map/ppermute | solution.py:29
  228.5 5.5 %collective-permute-start.8 = (f32[1,8,4,256]{3,2,1,0:T(4,128)S(1)}, f32[1,8,4,256]{3,2,1,0:T(4,128)S(1)}, u32[]{:S(2)}, u32[]{:S(2)}) collective-permute-start(f32[1,8,4,256]{3,2,1,0:T(4,128)S(1)} %get-tuple-element.62), channel_id=1, source_target_pairs={{0,5},{1,6},{2,7},{3,0},{4,1},{5,2},{6,3},{7,4},{8,13},{9,14},{10,... | collective-permute-start | bytes 98312 | tf_op jit(solution)/shard_map/ppermute | solution.py:29
  231.0 3.9 %collective-permute-start.9 = (f32[1,8,4,256]{3,2,1,0:T(4,128)S(1)}, f32[1,8,4,256]{3,2,1,0:T(4,128)S(1)}, u32[]{:S(2)}, u32[]{:S(2)}) collective-permute-start(f32[1,8,4,256]{3,2,1,0:T(4,128)S(1)} %get-tuple-element.61), channel_id=1, source_target_pairs={{0,6},{1,7},{2,0},{3,1},{4,2},{5,3},{6,4},{7,5},{8,14},{9,15},{10,... | collective-permute-start | bytes 98312 | tf_op jit(solution)/shard_map/ppermute | solution.py:29
  232.4 4.0 %collective-permute-start.10 = (f32[1,8,4,256]{3,2,1,0:T(4,128)S(1)}, f32[1,8,4,256]{3,2,1,0:T(4,128)S(1)}, u32[]{:S(2)}, u32[]{:S(2)}) collective-permute-start(f32[1,8,4,256]{3,2,1,0:T(4,128)S(1)} %get-tuple-element.60), channel_id=1, source_target_pairs={{0,7},{1,0},{2,1},{3,2},{4,3},{5,4},{6,5},{7,6},{8,15},{9,8},{10,9... | collective-permute-start | bytes 98312 | tf_op jit(solution)/shard_map/ppermute | solution.py:29
  (4 other events, 10.0 us)
Sparse Core Ops, SparseCore 0:
  194.3 26.1 reduce-scatter.1
